TPU v7x, 256 devices: a whole 4x4x8 slice. The times are simulated.
256 devices in a mesh: req: 32 (over y, x, core), tp: 8 (over z).
Axes of the slice: x: 4, y: 4, z: 8, core: 2. Of those that a mesh axis runs over, the one named last changes fastest.
Arguments:
- tokens: bfloat16 [256, 4, 1536], P('req'), may hold values from -6 to 6
- lengths: int32 [256], P('req'), may hold values from 16 to 32768, as said below
- page_table: int32 [256, 9], P('req'), may hold values from 0 to 2303, as said below
- kv_pages: bfloat16 [2304, 2, 128, 128], P('req'), may hold values from -480 to 480
- norm_gain: float32 [1536], replicated, may hold values from 0.1 to 1.9
- query_weight: bfloat16 [1536, 1024], P(None, 'tp'), may hold values from -0.15625 to 0.15625
- key_weight: bfloat16 [1536, 128], replicated, may hold values from -0.15625 to 0.15625
- value_weight: bfloat16 [1536, 128], replicated, may hold values from -0.15625 to 0.15625
- out_weight: bfloat16 [1024, 1536], P('tp'), may hold values from -0.1875 to 0.1875
- mlp_gain: float32 [1536], replicated, may hold values from 0.1 to 1.9
- gate_weight: bfloat16 [1536, 4608], P(None, 'tp'), may hold values from -0.15625 to 0.15625
- up_weight: bfloat16 [1536, 4608], P(None, 'tp'), may hold values from -0.15625 to 0.15625
- down_weight: bfloat16 [4608, 1536], P('tp'), may hold values from -0.09375 to 0.09375
Outputs:
- layer_out: bfloat16 [256, 4, 1536], P('req')
Inputs may be any that keep to these rules, and one draw needn't show every extreme that they name: `lengths`: one request has exactly 32768 cached positions in every draw. `page_table`: all entries together are a permutation of the 2304 pool pages. Entry (r, j) is pool page r * 9 + j, in the part of the pool held with request r, except for spilled entries chosen from the seed (about a fifth of all); the spilled entries hold one another's pool pages in an order drawn from the seed, mostly on other devices of req.
All inputs are finite; a program needn't handle non-finite values.
Results may differ from a plain program's by a relative error of at most 0.0095.
The roundings to bfloat16 on the way count: a program that leaves them out, or rounds other values in their place, can miss the bound.
Values may be sent and summed in bfloat16 or wider, within the bound.
No kernel may reach another device: no remote copies, remote signals or barrier semaphores. Data moves between devices by JAX's collectives and lax.ppermute only.
A program may use at most 128 MiB of HBM per device.

v0:
```python
import jax
import jax.numpy as jnp
from jax import lax
from jax.sharding import PartitionSpec as P

WINDOW = 1024
negative = -1e30
epsilon = 1e-06


def rms_norm(values, gain):
    return values * lax.rsqrt(jnp.mean(values * values, axis=-1, keepdims=True) + epsilon) * gain


def body(
    tokens,
    lengths,
    page_table,
    kv_pages,
    norm_gain,
    query_weight,
    key_weight,
    value_weight,
    out_weight,
    mlp_gain,
    gate_weight,
    up_weight,
    down_weight,
):
    req_dev, steps, width = tokens.shape
    head_dim = key_weight.shape[1]
    heads_dev = query_weight.shape[1] // head_dim
    pool_size = kv_pages.shape[0]
    page_size = kv_pages.shape[2]
    window_pages = page_table.shape[1]
    token_rows = tokens.reshape(req_dev * steps, width)
    normed = rms_norm(token_rows.astype(jnp.float32), norm_gain).astype(jnp.bfloat16)
    queries = (
        jnp.dot(normed, query_weight, preferred_element_type=jnp.float32) * head_dim ** (-0.5)
    ).astype(jnp.bfloat16)
    key_new = jnp.dot(normed, key_weight, preferred_element_type=jnp.float32).astype(jnp.bfloat16)
    value_new = jnp.dot(normed, value_weight, preferred_element_type=jnp.float32).astype(
        jnp.bfloat16
    )
    all_lengths, all_table = (
        lax.all_gather(lengths, "req", axis=0, tiled=True),
        lax.all_gather(page_table, "req", axis=0, tiled=True),
    )
    all_queries = lax.all_gather(
        queries.reshape(req_dev, steps, heads_dev * head_dim), "req", axis=0, tiled=True
    )
    requests = all_lengths.shape[0]
    flat_table = all_table.reshape(-1)
    local_slot = flat_table - lax.axis_index("req") * pool_size
    inside = (local_slot >= 0) & (local_slot < pool_size)
    owner_entry = (
        jnp.zeros((pool_size,), jnp.int32)
        .at[jnp.where(inside, local_slot, pool_size)]
        .set(jnp.arange(flat_table.shape[0], dtype=jnp.int32), mode="drop")
    )
    page_request = owner_entry // window_pages
    page_number = owner_entry % window_pages
    page_length = all_lengths[page_request]
    first_page = jnp.maximum(page_length - (WINDOW - 1), 0) // page_size
    position = (first_page + page_number)[:, None] * page_size + jnp.arange(
        page_size, dtype=jnp.int32
    )[None, :]
    current = page_length[:, None] + jnp.arange(steps, dtype=jnp.int32)[None, :]
    visible = (position[:, None, :] < page_length[:, None, None]) & (
        position[:, None, :] > current[:, :, None] - WINDOW
    )
    visible = visible[:, :, None, :]
    page_queries = all_queries[page_request]
    scores = jnp.einsum(
        "pqd,pkd->pqk", page_queries, kv_pages[:, 0], preferred_element_type=jnp.float32
    )
    scores = jnp.where(visible, scores.reshape(pool_size, steps, heads_dev, page_size), negative)
    block_max = jnp.max(scores, axis=-1)
    weights = jnp.where(visible, jnp.exp(scores - block_max[..., None]), 0.0)
    block_total = jnp.sum(weights, axis=-1)
    block_out = jnp.einsum(
        "pqk,pkd->pqd",
        weights.astype(jnp.bfloat16).reshape(pool_size, steps * heads_dev, page_size),
        kv_pages[:, 1],
        preferred_element_type=jnp.float32,
    )
    block_out = block_out.reshape(pool_size, steps, heads_dev, head_dim)
    request_max = jnp.maximum(
        jax.ops.segment_max(block_max, page_request, num_segments=requests), negative
    )
    start_row = lax.axis_index("req") * req_dev
    cache_max = lax.pmax(request_max, "req")
    scale = jnp.exp(block_max - cache_max[page_request])
    sent_out = jax.ops.segment_sum(
        block_out * scale[..., None], page_request, num_segments=requests
    )
    sent_total = jax.ops.segment_sum(block_total * scale, page_request, num_segments=requests)
    cache_out, cache_total = (
        lax.psum_scatter(sent_out, "req", scatter_dimension=0, tiled=True),
        lax.psum_scatter(sent_total, "req", scatter_dimension=0, tiled=True),
    )
    mine_max = lax.dynamic_slice_in_dim(cache_max, start_row, req_dev, 0)
    local_queries = queries.reshape(req_dev, steps, heads_dev, head_dim)
    new_scores = jnp.einsum(
        "rshd,rtd->rsht",
        local_queries,
        key_new.reshape(req_dev, steps, head_dim),
        preferred_element_type=jnp.float32,
    )
    causal = (jnp.arange(steps)[None, :] <= jnp.arange(steps)[:, None])[None, :, None, :]
    new_scores = jnp.where(causal, new_scores, negative)
    new_max = jnp.max(new_scores, axis=-1)
    new_weights = jnp.where(causal, jnp.exp(new_scores - new_max[..., None]), 0.0)
    new_total = jnp.sum(new_weights, axis=-1)
    new_out = jnp.einsum(
        "rsht,rtd->rshd",
        new_weights.astype(jnp.bfloat16),
        value_new.reshape(req_dev, steps, head_dim),
        preferred_element_type=jnp.float32,
    )
    overall = jnp.maximum(mine_max, new_max)
    cache_scale = jnp.exp(mine_max - overall)
    new_scale = jnp.exp(new_max - overall)
    total = cache_total * cache_scale + new_total * new_scale
    summed = cache_out * cache_scale[..., None] + new_out * new_scale[..., None]
    attended = (
        (summed / total[..., None])
        .astype(jnp.bfloat16)
        .reshape(req_dev * steps, heads_dev * head_dim)
    )
    projected = jnp.dot(attended, out_weight, preferred_element_type=jnp.float32)
    attn_total = lax.psum(projected, "tp")
    residual = (token_rows.astype(jnp.float32) + attn_total).astype(jnp.bfloat16)
    mlp_in = rms_norm(residual.astype(jnp.float32), mlp_gain).astype(jnp.bfloat16)
    gate = jnp.dot(mlp_in, gate_weight, preferred_element_type=jnp.float32)
    upward = jnp.dot(mlp_in, up_weight, preferred_element_type=jnp.float32)
    hidden = (jax.nn.gelu(gate, approximate=True) * upward).astype(jnp.bfloat16)
    mlp_total = lax.psum(
        jnp.dot(hidden, down_weight, preferred_element_type=jnp.float32).astype(jnp.bfloat16), "tp"
    ).astype(jnp.float32)
    layer_out = (residual.astype(jnp.float32) + mlp_total).astype(jnp.bfloat16)
    return layer_out.reshape(req_dev, steps, width)


def solution(mesh):
    return jax.shard_map(
        body,
        mesh=mesh,
        in_specs=(
            P("req", None, None),
            P("req"),
            P("req", None),
            P("req", None, None, None),
            P(),
            P(None, "tp"),
            P(),
            P(),
            P("tp", None),
            P(),
            P(None, "tp"),
            P(None, "tp"),
            P("tp", None),
        ),
        out_specs=P("req", None, None),
        check_vma=False,
    )
```

profile of v0, /device:TPU:2, one launch (start us, length us, event | category | flops | bytes accessed | tf_op | source)
XLA Modules:
  0.0 512.9 jit_solution(16299514413610461038)
XLA Ops:
  6.5 0.0 copy-start
  6.5 0.0 reduce-scatter.6.cloned.1.call-start
  6.5 1.4 fusion.63
  8.6 0.9 dynamic-update-slice
  9.5 15.7 %all-reduce = s32[256]{0:T(256)S(1)} all-reduce(s32[256]{0:T(256)S(1)} %dynamic-update-slice), channel_id=1, replica_groups=mesh['req'=32,'tp'=8] {'req'}, use_global_device_ids=true, to_apply=%add | all-reduce | flops 256 | bytes 2048
  25.2 23.4 %all_gather.9 = s32[256,9]{1,0:T(8,128)S(1)} all-gather(s32[8,9]{1,0:T(8,128)} %param.15), channel_id=1, replica_groups=mesh['req'=32,'tp'=8] {'req'}, dimensions={0}, use_global_device_ids=true | all-gather | bytes 9504 | tf_op jit(solution)/shard_map/all_gather | solution.py:47
  48.5 0.2 sub.78
  48.8 9.0 %scatter_custom_fusion = s32[72]{0:T(128)S(1)} fusion(s32[2304]{0:T(1024)S(1)} %fusion.44, s32[2304]{0:T(1024)S(1)} %iota.34, s32[]{:T(128)} %constant.27.clone.1), kind=kCustom, calls=%fused_computation.93 | custom fusion | bytes 292 | tf_op jit(solution)/shard_map/scatter | solution.py:59
  57.8 1.3 gather_fusion
  59.1 0.1 broadcast_compare_fusion
  59.2 0.0 copy-start.8
  59.2 0.1 iota_add_fusion
  59.3 0.1 add_add_fusion
  59.4 1.0 multiply_reduce_fusion
  60.4 0.9 reshape.246
  61.4 0.1 rsqrt.20
  61.4 0.8 multiply_convert_fusion
  62.2 0.0 copy-done.2
  62.2 0.2 fusion.14
  62.4 22.6 %all_gather.11 = bf16[256,4,128]{2,1,0:T(4,128)(2,1)S(1)} all-gather(bf16[8,4,128]{2,1,0:T(4,128)(2,1)S(1)} %bitcast.89), channel_id=1, replica_groups=mesh['req'=32,'tp'=8] {'req'}, dimensions={0}, use_global_device_ids=true | all-gather | bytes 270336 | tf_op jit(solution)/shard_map/all_gather | solution.py:49
  85.0 0.7 gather_fusion.1
  85.7 3.1 fusion.64
  88.8 1.0 scatter_custom_fusion.1
  89.8 123.3 %pmax.7 = f32[256,4,1]{1,0,2:T(8,128)S(1)} all-reduce(f32[256,4,1]{1,0,2:T(8,128)S(1)} %maximum_bitcast_fusion), channel_id=1, replica_groups=mesh['req'=32,'tp'=8] {'req'}, use_global_device_ids=true, to_apply=%region_4.5 | all-reduce | flops 1024 | bytes 8192 | tf_op jit(solution)/shard_map/pmax | solution.py:92
  213.1 0.6 gather_fusion.2
  213.7 0.0 copy-start.6
  213.8 0.0 copy-done.8
  213.8 0.0 copy-done.4
  213.8 2.5 fusion.9
  216.3 0.1 broadcast.190
  216.3 0.0 copy-done.6
  216.3 3.5 scatter_fusion
  219.8 0.0 copy-start.1
  219.8 0.8 copy.86
  220.7 0.0 reduce-scatter.6.cloned.1.call-update
  220.7 0.0 copy-start.9
  220.7 0.0 all-reduce.5.cloned.1.call-start
  220.8 0.0 copy-done.3
  220.8 0.2 convolution_convert_fusion.2
  221.0 0.1 fusion.65
  221.1 0.1 copy.56
  221.2 0.1 select_reduce_fusion
  221.3 0.1 copy.59
  221.4 0.1 fusion.45
  221.5 0.1 copy.81
  221.6 0.1 copy.63
  221.7 1.3 fusion.57
  222.9 1.2 scatter_custom_fusion.3
  224.7 123.8 %all-reduce.1 = f32[256,4,1]{1,0,2:T(8,128)S(1)} all-reduce(f32[256,4,1]{1,0,2:T(8,128)S(1)} %bitcast.88), channel_id=3, replica_groups=mesh['req'=32,'tp'=8] {'req'}, use_global_device_ids=true, to_apply=%region_10.11.clone | all-reduce | flops 1024 | bytes 8192
  348.6 1.2 convolution_convert_fusion.1
  349.8 0.0 reduce-scatter.6.cloned.1.call-done
  349.8 0.7 reshape.332
  350.5 0.1 fusion.17
  350.7 0.9 fusion.66
  351.5 0.0 all-reduce.5.cloned.1.call-update
  351.6 0.0 all-reduce.7.cloned.1.call-start
  351.6 75.7 %all-reduce.5.cloned.1.call-done = f32[32,1536]{1,0:T(8,128)} async-done(((f32[32,1536]{1,0:T(8,128)}), f32[32,1536]{1,0:T(8,128)}) %all-reduce.5.cloned.1.call-update) | async-done | bytes 196624 | tf_op jit(solution)/shard_map/psum | solution.py:132
  427.3 1.1 fusion.18
  428.4 2.1 fusion.42
  430.5 3.2 convolution_convert_fusion
  433.7 0.0 all-reduce.7.cloned.1.call-update
  433.7 71.0 %all-reduce.7.cloned.1.call-done = bf16[32,1536]{1,0:T(8,128)(2,1)} async-done(((bf16[32,1536]{1,0:T(8,128)(2,1)}), bf16[32,1536]{1,0:T(8,128)(2,1)}) %all-reduce.7.cloned.1.call-update) | async-done | bytes 98320 | tf_op jit(solution)/shard_map/psum | solution.py:138
  504.8 0.9 fusion.21
  505.7 0.7 reshape.245
  (23 shorter events, 0.2 us)
Async XLA Ops:
  6.5 424.0 %copy-start = (bf16[576,1536]{1,0:T(8,128)(2,1)S(1)}, bf16[576,1536]{1,0:T(8,128)(2,1)}, u32[]{:S(2)}) copy-start(bf16[576,1536]{1,0:T(8,128)(2,1)} %param.25) | copy-start | bytes 5308420
  6.5 55.7 %copy-start.2 = (bf16[1536,128]{1,0:T(8,128)(2,1)S(1)}, bf16[1536,128]{1,0:T(8,128)(2,1)}, u32[]{:S(2)}) copy-start(bf16[1536,128]{1,0:T(8,128)(2,1)} %param.18) | copy-start | bytes 1179652
  6.5 343.3 %reduce-scatter.6.cloned.1.call-start = ((), (), s32[]{:S(2)}) async-start(), calls=%async_computation.3 | async-start | bytes 540672
  59.2 154.5 %copy-start.8 = (pred[72,128]{1,0:T(8,128)(4,1)}, pred[72,128]{1,0:T(8,128)(4,1)S(1)}, u32[]{:S(2)}) copy-start(pred[72,128]{1,0:T(8,128)(4,1)S(1)} %broadcast_compare_fusion) | copy-start | bytes 27652
  59.3 154.5 %copy-start.4 = (s32[72,128]{1,0:T(8,128)}, s32[72,128]{1,0:T(8,128)S(1)}, u32[]{:S(2)}) copy-start(s32[72,128]{1,0:T(8,128)S(1)} %iota_add_fusion) | copy-start | bytes 110596
  59.4 154.4 %copy-start.5 = (s32[72,4]{1,0:T(8,128)}, s32[72,4]{1,0:T(8,128)S(1)}, u32[]{:S(2)}) copy-start(s32[72,4]{1,0:T(8,128)S(1)} %add_add_fusion) | copy-start | bytes 3460
  88.8 125.0 %copy-start.7 = (f32[72,4,128]{2,1,0:T(4,128)}, f32[72,4,128]{2,1,0:T(4,128)S(1)}, u32[]{:S(2)}) copy-start(f32[72,4,128]{2,1,0:T(4,128)S(1)} %get-tuple-element.17) | copy-start | bytes 442372
  213.7 2.6 copy-start.6
  216.3 4.5 copy-start.3
  219.8 130.8 %copy-start.1 = (bf16[128,1536]{1,0:T(8,128)(2,1)S(1)}, bf16[128,1536]{1,0:T(8,128)(2,1)}, u32[]{:S(2)}) copy-start(bf16[128,1536]{1,0:T(8,128)(2,1)} %param.21) | copy-start | bytes 1179652
  220.7 207.7 %copy-start.9 = (f32[1536]{0:T(1024)S(1)}, f32[1536]{0:T(1024)}, u32[]{:S(2)}) copy-start(f32[1536]{0:T(1024)} %param.22) | copy-start | bytes 18436
  220.7 206.6 %all-reduce.5.cloned.1.call-start = ((), (), s32[]{:S(2)}) async-start(), calls=%async_computation.1 | async-start | bytes 393216 | tf_op jit(solution)/shard_map/psum | solution.py:132
  351.6 153.2 %all-reduce.7.cloned.1.call-start = ((), (), s32[]{:S(2)}) async-start(), calls=%async_computation.2 | async-start | bytes 196608 | tf_op jit(solution)/shard_map/psum | solution.py:138
Sparse Core Ops, SparseCore 0:
  220.8 87.7 reduce-scatter.5
  351.7 75.5 all-reduce.4
  433.8 70.8 all-reduce.6
where the time goes:
time: 514 us; the launch traced here: 513 us
  blocking collectives  309 us (60%)
  waiting for transfers between devices  147 us (29%)
  local copies, waits for them, and re-layouts  17.7 us (3%)
  between operations  14.6 us (3%)
  matrix products  13.5 us (3%)
  other arithmetic  11.4 us (2%)
    unnamed x2, blocking collectives  140 us
    pmax x1, blocking collectives, body(): cache_max = lax.pmax(request_max, 'req')  123 us
    psum x1, waiting for transfers between devices, body(): attn_total = lax.psum(projected, 'tp')  75.7 us
    psum x1, waiting for transfers between devices, body(): lax.psum(jnp.dot(hidden, down_weight, preferred_element_type=jnp.float32)...  71 us
    all_gather x1, blocking collectives, body(): lax.all_gather(page_table, 'req', axis=0, tiled=True)  23.4 us
    all_gather x1, blocking collectives, body(): lax.all_gather(queries.reshape(req_dev, steps, heads_dev * head_dim), 're...  22.6 us
  transfers between devices with their start and end apart: 3, of which 2 were waited for; matrix products, arithmetic and copies ran while one was open for 1% of the time, Pallas kernels for 0%

commit v1 on v0

--- a/solution.py
+++ b/solution.py
@@ -129,7 +129,11 @@
         .reshape(req_dev * steps, heads_dev * head_dim)
     )
     projected = jnp.dot(attended, out_weight, preferred_element_type=jnp.float32)
-    attn_total = lax.psum(projected, "tp")
+    attn_total = projected
+    for hop in (1, 2, 4):
+        attn_total = attn_total + lax.ppermute(
+            attn_total, "tp", [(dev, dev ^ hop) for dev in range(8)]
+        )
     residual = (token_rows.astype(jnp.float32) + attn_total).astype(jnp.bfloat16)
     mlp_in = rms_norm(residual.astype(jnp.float32), mlp_gain).astype(jnp.bfloat16)
     gate = jnp.dot(mlp_in, gate_weight, preferred_element_type=jnp.float32)

time: 514 us -> 475 us (0.924)
  waiting for transfers between devices: 147 us -> 93.2 us
  starting transfers between devices: 0.09 us -> 11.5 us
    psum x1 -> x0, waiting for transfers between devices: 75.7 us -> none  [body(): attn_total = lax.psum(projected, 'tp')]
    ppermute x0 -> x3, waiting for transfers between devices: none -> 19 us  [body(): lax.ppermute(attn_total, 'tp', [(dev, dev ^ hop) for dev in range(8)])]
    ppermute x0 -> x3, starting transfers between devices: none -> 11.5 us  [body(): lax.ppermute(attn_total, 'tp', [(dev, dev ^ hop) for dev in range(8)])]
  transfers between devices with their start and end apart: 3 -> 5, of which waited for: 2 -> 4; matrix products, arithmetic and copies ran while one was open for 1% -> 1% of each run, Pallas kernels for 0% -> 0%
where the time goes in v1:
time: 475 us; the launch traced here: 474 us
  blocking collectives  310 us (65%)
  waiting for transfers between devices  93.2 us (20%)
  local copies, waits for them, and re-layouts  19.6 us (4%)
  between operations  15.1 us (3%)
  matrix products  13.8 us (3%)
  starting transfers between devices  11.5 us (2%)
  other arithmetic  11.2 us (2%)
    unnamed x2, blocking collectives  141 us
    pmax x1, blocking collectives, body(): cache_max = lax.pmax(request_max, 'req')  123 us
    psum x1, waiting for transfers between devices, body(): lax.psum(jnp.dot(hidden, down_weight, preferred_element_type=jnp.float32)...  74.1 us
    all_gather x1, blocking collectives, body(): lax.all_gather(page_table, 'req', axis=0, tiled=True)  23.4 us
    all_gather x1, blocking collectives, body(): lax.all_gather(queries.reshape(req_dev, steps, heads_dev * head_dim), 're...  22.6 us
    ppermute x3, waiting for transfers between devices, body(): lax.ppermute(attn_total, 'tp', [(dev, dev ^ hop) for dev in range(8)])  19 us
    ppermute x3, starting transfers between devices, body(): lax.ppermute(attn_total, 'tp', [(dev, dev ^ hop) for dev in range(8)])  11.5 us
  transfers between devices with their start and end apart: 5, of which 4 were waited for; matrix products, arithmetic and copies ran while one was open for 1% of the time, Pallas kernels for 0%

profile of v1, /device:TPU:2, one launch (start us, length us, event | category | flops | bytes accessed | tf_op | source)
XLA Modules:
  0.0 474.2 jit_solution(17992276218561833858)
XLA Ops:
  6.5 0.0 copy-start
  6.5 1.5 fusion.63
  8.7 0.9 dynamic-update-slice
  9.5 15.7 %all-reduce = s32[256]{0:T(256)S(1)} all-reduce(s32[256]{0:T(256)S(1)} %dynamic-update-slice), channel_id=1, replica_groups=mesh['req'=32,'tp'=8] {'req'}, use_global_device_ids=true, to_apply=%add | all-reduce | flops 256 | bytes 2048
  25.2 23.4 %all_gather.9 = s32[256,9]{1,0:T(8,128)S(1)} all-gather(s32[8,9]{1,0:T(8,128)} %param.15), channel_id=1, replica_groups=mesh['req'=32,'tp'=8] {'req'}, dimensions={0}, use_global_device_ids=true | all-gather | bytes 9504 | tf_op jit(solution)/shard_map/all_gather | solution.py:47
  48.6 0.2 sub.78
  48.8 9.0 %scatter_custom_fusion = s32[72]{0:T(128)S(1)} fusion(s32[2304]{0:T(1024)S(1)} %fusion.44, s32[2304]{0:T(1024)S(1)} %iota.34, s32[]{:T(128)} %constant.27.clone.1), kind=kCustom, calls=%fused_computation.93 | custom fusion | bytes 292 | tf_op jit(solution)/shard_map/scatter | solution.py:59
  57.9 1.3 gather_fusion
  59.1 0.1 broadcast_compare_fusion
  59.2 0.1 iota_add_fusion
  59.3 0.1 add_add_fusion
  59.4 1.0 multiply_reduce_fusion
  60.4 0.9 reshape.246
  61.4 0.1 rsqrt.20
  61.4 0.8 multiply_convert_fusion
  62.2 0.0 copy-start.6
  62.3 0.2 fusion.14
  62.4 22.6 %all_gather.11 = bf16[256,4,128]{2,1,0:T(4,128)(2,1)S(1)} all-gather(bf16[8,4,128]{2,1,0:T(4,128)(2,1)S(1)} %bitcast.89), channel_id=1, replica_groups=mesh['req'=32,'tp'=8] {'req'}, dimensions={0}, use_global_device_ids=true | all-gather | bytes 270336 | tf_op jit(solution)/shard_map/all_gather | solution.py:49
  85.1 0.7 gather_fusion.1
  85.7 3.1 fusion.64
  88.8 1.0 scatter_custom_fusion.1
  89.8 123.3 %pmax.7 = f32[256,4,1]{1,0,2:T(8,128)S(1)} all-reduce(f32[256,4,1]{1,0,2:T(8,128)S(1)} %maximum_bitcast_fusion), channel_id=1, replica_groups=mesh['req'=32,'tp'=8] {'req'}, use_global_device_ids=true, to_apply=%region_4.5 | all-reduce | flops 1024 | bytes 8192 | tf_op jit(solution)/shard_map/pmax | solution.py:92
  213.1 0.6 gather_fusion.2
  213.8 0.0 copy-done.7
  213.8 2.5 fusion.9
  216.2 0.1 broadcast.190
  216.3 3.5 scatter_fusion
  219.8 0.8 copy.86
  220.6 0.0 reduce-scatter.6.cloned.1.call-update
  220.6 0.0 all-reduce.4.cloned.1.call-start
  220.7 0.2 convolution_convert_fusion.2
  220.9 0.1 fusion.65
  221.0 0.1 copy.56
  221.1 0.1 select_reduce_fusion
  221.2 0.1 copy.59
  221.3 0.1 fusion.45
  221.4 0.1 copy.81
  221.5 0.7 copy.63
  222.2 0.3 fusion.57
  222.6 1.6 scatter_custom_fusion.3
  224.9 125.0 %all-reduce.1 = f32[256,4,1]{1,0,2:T(8,128)} all-reduce(f32[256,4,1]{1,0,2:T(8,128)} %bitcast.88), channel_id=3, replica_groups=mesh['req'=32,'tp'=8] {'req'}, use_global_device_ids=true, to_apply=%region_10.11.clone | all-reduce | flops 1024 | bytes 8192
  349.9 1.3 fusion.52
  351.2 1.2 convolution_convert_fusion.1
  352.5 0.0 reduce-scatter.6.cloned.1.call-done
  352.5 1.3 reshape.332
  353.8 0.9 fusion.17
  354.7 1.2 fusion.66
  355.9 2.1 collective-permute-start
  357.9 5.4 %collective-permute-done = f32[32,1536]{1,0:T(8,128)S(1)} collective-permute-done((f32[32,1536]{1,0:T(8,128)S(1)}, f32[32,1536]{1,0:T(8,128)S(1)}, u32[]{:S(2)}, u32[]{:S(2)}) %collective-permute-start) | collective-permute-done | bytes 196640 | tf_op jit(solution)/shard_map/ppermute | solution.py:134
  363.3 3.0 collective-permute-start.1
  366.3 10.0 %collective-permute-done.1 = f32[32,1536]{1,0:T(8,128)S(1)} collective-permute-done((f32[32,1536]{1,0:T(8,128)S(1)}, f32[32,1536]{1,0:T(8,128)S(1)}, u32[]{:S(2)}, u32[]{:S(2)}) %collective-permute-start.1) | collective-permute-done | bytes 196640 | tf_op jit(solution)/shard_map/ppermute | solution.py:134
  376.3 6.4 %collective-permute-start.2 = (f32[32,1536]{1,0:T(8,128)S(1)}, f32[32,1536]{1,0:T(8,128)S(1)}, u32[]{:S(2)}, u32[]{:S(2)}) collective-permute-start(f32[32,1536]{1,0:T(8,128)S(1)} %add.145), channel_id=1, source_target_pairs={{0,4},{1,5},{2,6},{3,7},{4,0},{5,1},{6,2},{7,3},{8,12},{9,13},{10,... | collective-permute-start | bytes 589832 | tf_op jit(solution)/shard_map/ppermute | solution.py:134
  382.7 3.6 collective-permute-done.2
  386.4 0.1 fusion.18
  386.5 0.6 copy-done.4
  387.2 0.0 copy-done.10
  387.2 1.3 fusion.42
  388.5 0.0 copy-done
  388.5 3.2 convolution_convert_fusion
  391.6 0.0 all-reduce.4.cloned.1.call-update
  391.7 74.1 %all-reduce.4.cloned.1.call-done = bf16[32,1536]{1,0:T(8,128)(2,1)} async-done(((bf16[32,1536]{1,0:T(8,128)(2,1)}), bf16[32,1536]{1,0:T(8,128)(2,1)}) %all-reduce.4.cloned.1.call-update) | async-done | bytes 98320 | tf_op jit(solution)/shard_map/psum | solution.py:142
  465.8 0.0 copy-done.5
  465.8 0.9 fusion.21
  466.7 0.7 reshape.245
  (30 shorter events, 0.2 us)
Async XLA Ops:
  6.5 381.9 %copy-start = (bf16[576,1536]{1,0:T(8,128)(2,1)S(1)}, bf16[576,1536]{1,0:T(8,128)(2,1)}, u32[]{:S(2)}) copy-start(bf16[576,1536]{1,0:T(8,128)(2,1)} %param.25) | copy-start | bytes 5308420
  6.5 55.7 %copy-start.8 = (bf16[1536,128]{1,0:T(8,128)(2,1)S(1)}, bf16[1536,128]{1,0:T(8,128)(2,1)}, u32[]{:S(2)}) copy-start(bf16[1536,128]{1,0:T(8,128)(2,1)} %param.18) | copy-start | bytes 1179652
  6.5 345.9 %reduce-scatter.6.cloned.1.call-start = ((), (), s32[]{:S(2)}) async-start(), calls=%async_computation.2 | async-start | bytes 540672
  61.3 27.5 %copy-start.2 = (f32[32,1536]{1,0:T(8,128)}, f32[32,1536]{1,0:T(8,128)S(1)}, u32[]{:S(2)}) copy-start(f32[32,1536]{1,0:T(8,128)S(1)} %reshape.246) | copy-start | bytes 589828
  62.2 158.5 %copy-start.6 = (bf16[32,1536]{1,0:T(8,128)(2,1)}, bf16[32,1536]{1,0:T(8,128)(2,1)S(1)}, u32[]{:S(2)}) copy-start(bf16[32,1536]{1,0:T(8,128)(2,1)S(1)} %multiply_convert_fusion) | copy-start | bytes 294916
  213.1 0.6 copy-start.7
  216.2 4.5 copy-start.9
  220.6 245.2 %all-reduce.4.cloned.1.call-start = ((), (), s32[]{:S(2)}) async-start(), calls=%async_computation.1 | async-start | bytes 196608 | tf_op jit(solution)/shard_map/psum | solution.py:142
  224.2 163.0 %copy-start.1 = (bf16[1536,576]{0,1:T(8,128)(2,1)S(1)}, bf16[1536,576]{0,1:T(8,128)(2,1)}, u32[]{:S(2)}) copy-start(bf16[1536,576]{0,1:T(8,128)(2,1)} %param.23) | copy-start | bytes 5308420
  224.2 163.0 %copy-start.10 = (f32[1536]{0:T(1024)S(1)}, f32[1536]{0:T(1024)}, u32[]{:S(2)}) copy-start(f32[1536]{0:T(1024)} %param.22) | copy-start | bytes 18436
  353.8 32.6 %copy-start.3 = (f32[32,1536]{1,0:T(8,128)S(1)}, f32[32,1536]{1,0:T(8,128)}, u32[]{:S(2)}) copy-start(f32[32,1536]{1,0:T(8,128)} %copy-done.2) | copy-start | bytes 589828
  355.9 7.4 %collective-permute-start = (f32[32,1536]{1,0:T(8,128)S(1)}, f32[32,1536]{1,0:T(8,128)S(1)}, u32[]{:S(2)}, u32[]{:S(2)}) collective-permute-start(f32[32,1536]{1,0:T(8,128)S(1)} %fusion.66), channel_id=1, source_target_pairs={{0,1},{1,0},{2,3},{3,2},{4,5},{5,4},{6,7},{7,6},{8,9},{9,8},{10,11... | collective-permute-start | bytes 589832 | tf_op jit(solution)/shard_map/ppermute | solution.py:134
  363.3 13.0 %collective-permute-start.1 = (f32[32,1536]{1,0:T(8,128)S(1)}, f32[32,1536]{1,0:T(8,128)S(1)}, u32[]{:S(2)}, u32[]{:S(2)}) collective-permute-start(f32[32,1536]{1,0:T(8,128)S(1)} %add.144), channel_id=1, source_target_pairs={{0,2},{1,3},{2,0},{3,1},{4,6},{5,7},{6,4},{7,5},{8,10},{9,11},{10,... | collective-permute-start | bytes 589832 | tf_op jit(solution)/shard_map/ppermute | solution.py:134
  376.3 10.0 %collective-permute-start.2 = (f32[32,1536]{1,0:T(8,128)S(1)}, f32[32,1536]{1,0:T(8,128)S(1)}, u32[]{:S(2)}, u32[]{:S(2)}) collective-permute-start(f32[32,1536]{1,0:T(8,128)S(1)} %add.145), channel_id=1, source_target_pairs={{0,4},{1,5},{2,6},{3,7},{4,0},{5,1},{6,2},{7,3},{8,12},{9,13},{10,... | collective-permute-start | bytes 589832 | tf_op jit(solution)/shard_map/ppermute | solution.py:134
  386.5 0.6 copy-start.4
  388.5 77.3 %copy-start.5 = (bf16[32,1536]{1,0:T(8,128)(2,1)S(1)}, bf16[32,1536]{1,0:T(8,128)(2,1)}, u32[]{:S(2)}) copy-start(bf16[32,1536]{1,0:T(8,128)(2,1)} %copy-done.4) | copy-start | bytes 294916
Sparse Core Ops, SparseCore 0:
  220.8 87.7 reduce-scatter.5
  391.8 73.9 all-reduce.3
